TPU v7x, 32 devices: a whole 2x2x4 slice. The times are simulated.
32 devices in a mesh: dp: 8 (over z, x), tensor: 4 (over y, core).
Axes of the slice: x: 2, y: 2, z: 4, core: 2. Of those that a mesh axis runs over, the one named last changes fastest.
Arguments:
- tokens: bfloat16 [2048, 4096], P('dp', 'tensor'), may hold values from -6 to 6
- norm_gain: float32 [4096], replicated, may hold values from 0.15 to 5.4, as said below
- w_query: bfloat16 [4096, 4096], P(None, 'tensor'), may hold values from -0.09375 to 0.09375
- key_weight: bfloat16 [4096, 1024], P(None, 'tensor'), may hold values from -0.09375 to 0.09375
- value_weight: bfloat16 [4096, 1024], P(None, 'tensor'), may hold values from -0.09375 to 0.09375
- w_out: bfloat16 [4096, 4096], P('tensor'), may hold values from -0.25 to 0.25
- grad_output: bfloat16 [2048, 4096], P('dp', 'tensor'), may hold values from -6 to 6
- doc_lengths: int32 [8, 2], P('dp'), may hold values from 0 to 256, as said below
- block_owner: int32 [8, 8], replicated, may hold values from 0 to 7, as said below
Outputs:
- relaid_output: bfloat16 [2048, 4096], P('dp', 'tensor')
- input_grad: bfloat16 [2048, 4096], P('dp', 'tensor')
Inputs may be any that keep to these rules, and one draw needn't show every extreme that they name: `doc_lengths`: each row lists the lengths of the documents packed on that dp index in order: multiples of 128, the nonzero ones first, summing to 256. In every draw some dp index holds a single document of 256 tokens. `block_owner`: every dp index owns exactly one block of each position j < 8 and exactly one block from each dp index. `norm_gain`: positive gains.
All inputs are finite; a program needn't handle non-finite values.
Results may differ from a plain program's by a relative error of at most 0.015.
Values may be sent and summed in bfloat16 or wider, within the bound.
No kernel may reach another device: no remote copies, remote signals or barrier semaphores. Data moves between devices by JAX's collectives and lax.ppermute only.
A program may use at most 128 MiB of HBM per device.

v0:
```python
import math
import jax
import jax.numpy as jnp
from jax import lax
from jax.sharding import PartitionSpec as P

HEAD_SIZE = 128
ROPE_BASE = 500000.0
NORM_EPSILON = 1e-05


def doc_tables(lengths_row, token_row_count):
    ends = jnp.cumsum(lengths_row)
    token_index = jnp.arange(token_row_count, dtype=jnp.int32)
    passed = (token_index[:, None] >= ends[None, :]).astype(jnp.int32)
    doc_ids = jnp.sum(passed, axis=1)
    starts = jnp.max(jnp.where(passed > 0, ends[None, :], 0), axis=1)
    return (doc_ids, token_index - starts)


def rope_tables(positions, head_size):
    half_dim = head_size // 2
    steps = jnp.arange(half_dim, dtype=jnp.float32)
    inverse_freq = jnp.power(ROPE_BASE, -2.0 * steps / head_size)
    angles = positions.astype(jnp.float32)[:, None] * inverse_freq[None, :]
    return (jnp.cos(angles), jnp.sin(angles))


def rotate(vectors, cosine, sine_table):
    half_dim = vectors.shape[-1] // 2
    former = vectors[..., :half_dim]
    latter = vectors[..., half_dim:]
    cos_part = cosine[:, None, :]
    sin_part = sine_table[:, None, :]
    return jnp.concatenate(
        [former * cos_part - latter * sin_part, latter * cos_part + former * sin_part], axis=-1
    )


def unrotate(vectors, cosine, sine_table):
    half_dim = vectors.shape[-1] // 2
    former = vectors[..., :half_dim]
    latter = vectors[..., half_dim:]
    cos_part = cosine[:, None, :]
    sin_part = sine_table[:, None, :]
    return jnp.concatenate(
        [former * cos_part + latter * sin_part, latter * cos_part - former * sin_part], axis=-1
    )


def per_device(
    tokens,
    norm_gain,
    w_query,
    key_weight,
    value_weight,
    w_out,
    grad_output,
    doc_lengths,
    block_owner,
):
    token_row_count, width_part = tokens.shape
    full_width = norm_gain.shape[0]
    sources = lax.axis_size("dp")
    data_index = lax.axis_index("dp")
    tensor_index = lax.axis_index("tensor")
    query_width = w_query.shape[1]
    key_width = key_weight.shape[1]
    heads_local = query_width // HEAD_SIZE
    kv_local = key_width // HEAD_SIZE
    query_group_width = heads_local // kv_local
    scale_factor = 1.0 / math.sqrt(HEAD_SIZE)
    gain_part = lax.dynamic_slice_in_dim(norm_gain, tensor_index * width_part, width_part)
    w_joined = jnp.concatenate([w_query, key_weight, value_weight], axis=1)
    x_float = tokens.astype(jnp.float32)
    gathered = lax.all_gather(tokens, "tensor", axis=1, tiled=True)
    gathered_float = gathered.astype(jnp.float32)
    inverse = lax.rsqrt(jnp.mean(gathered_float * gathered_float, axis=1) + NORM_EPSILON)
    normed_input = (gathered_float * inverse[:, None] * norm_gain[None, :]).astype(jnp.bfloat16)
    projected = jnp.dot(normed_input, w_joined, preferred_element_type=jnp.float32)
    doc_ids, positions = doc_tables(doc_lengths[0], token_row_count)
    token_index = jnp.arange(token_row_count, dtype=jnp.int32)
    allowed = (doc_ids[:, None] == doc_ids[None, :]) & (
        token_index[None, :] <= token_index[:, None]
    )
    cosine, sine_table = rope_tables(positions, HEAD_SIZE)
    query_rows = rotate(
        projected[:, :query_width].reshape(token_row_count, heads_local, HEAD_SIZE),
        cosine,
        sine_table,
    ).astype(jnp.bfloat16)
    keys = rotate(
        projected[:, query_width : query_width + key_width].reshape(
            token_row_count, kv_local, HEAD_SIZE
        ),
        cosine,
        sine_table,
    ).astype(jnp.bfloat16)
    value_rows = (
        projected[:, query_width + key_width :]
        .astype(jnp.bfloat16)
        .reshape(token_row_count, kv_local, HEAD_SIZE)
    )
    grouped_query = query_rows.reshape(token_row_count, kv_local, query_group_width, HEAD_SIZE)
    scores = (
        jnp.einsum("qkgd,skd->kgqs", grouped_query, keys, preferred_element_type=jnp.float32)
        * scale_factor
    )
    weights = jnp.where(allowed[None, None], jnp.exp(scores), 0.0)
    probs = weights / jnp.sum(weights, axis=-1, keepdims=True)
    probs_low = probs.astype(jnp.bfloat16)
    attended = jnp.einsum(
        "kgqs,skd->qkgd", probs_low, value_rows, preferred_element_type=jnp.float32
    ).astype(jnp.bfloat16)
    attended_flat = attended.reshape(token_row_count, query_width)
    mixed_turned = lax.psum_scatter(
        lax.dot_general(
            w_out, attended_flat, (((0,), (1,)), ((), ())), preferred_element_type=jnp.float32
        ).astype(jnp.bfloat16),
        "tensor",
        scatter_dimension=0,
        tiled=True,
    ).astype(jnp.float32)
    output_home = (x_float + mixed_turned.T).astype(jnp.bfloat16)
    block_count = block_owner.shape[1]
    owner_row = lax.dynamic_slice_in_dim(block_owner, data_index, 1, 0)[0]
    slot_index = jnp.arange(sources, dtype=jnp.int32)
    send_table = (owner_row[None, :] == slot_index[:, None]).astype(jnp.bfloat16)
    owned_flags = jnp.sum((block_owner == data_index).astype(jnp.int32), axis=1)
    owned_rank = jnp.cumsum(owned_flags) - owned_flags
    block_index = jnp.arange(block_count, dtype=jnp.int32)
    keep_table = (
        (owned_rank[None, :] == block_index[:, None]) & (owned_flags[None, :] > 0)
    ).astype(jnp.bfloat16)
    home_blocks = output_home.reshape(block_count, -1)
    outgoing = jnp.dot(send_table, home_blocks, preferred_element_type=jnp.float32).astype(
        jnp.bfloat16
    )
    incoming = lax.all_to_all(outgoing, "dp", split_axis=0, concat_axis=0, tiled=True)
    relaid = (
        jnp.dot(keep_table, incoming, preferred_element_type=jnp.float32)
        .astype(jnp.bfloat16)
        .reshape(token_row_count, width_part)
    )
    owned_blocks = grad_output.reshape(block_count, -1)
    returning = lax.dot_general(
        keep_table, owned_blocks, (((0,), (0,)), ((), ())), preferred_element_type=jnp.float32
    ).astype(jnp.bfloat16)
    arrived = lax.all_to_all(returning, "dp", split_axis=0, concat_axis=0, tiled=True)
    grad_home = (
        lax.dot_general(
            send_table, arrived, (((0,), (0,)), ((), ())), preferred_element_type=jnp.float32
        )
        .astype(jnp.bfloat16)
        .reshape(token_row_count, width_part)
    )
    attended_gradient = lax.dot_general(
        lax.all_gather(grad_home, "tensor", axis=1, tiled=True),
        w_out,
        (((1,), (1,)), ((), ())),
        preferred_element_type=jnp.float32,
    ).astype(jnp.bfloat16)
    grouped_gradient = attended_gradient.reshape(
        token_row_count, kv_local, query_group_width, HEAD_SIZE
    )
    delta = jnp.sum(grouped_gradient.astype(jnp.float32) * attended.astype(jnp.float32), axis=-1)
    grad_probs = jnp.einsum(
        "qkgd,skd->kgqs", grouped_gradient, value_rows, preferred_element_type=jnp.float32
    )
    grad_scores = (probs * (grad_probs - jnp.transpose(delta, (1, 2, 0))[..., None])).astype(
        jnp.bfloat16
    )
    grad_query_rot = (
        jnp.einsum("kgqs,skd->qkgd", grad_scores, keys, preferred_element_type=jnp.float32)
        * scale_factor
    )
    grad_keys_rot = (
        jnp.einsum("kgqs,qkgd->skd", grad_scores, grouped_query, preferred_element_type=jnp.float32)
        * scale_factor
    )
    value_gradient = jnp.einsum(
        "kgqs,qkgd->skd", probs_low, grouped_gradient, preferred_element_type=jnp.float32
    )
    grad_query = unrotate(
        grad_query_rot.reshape(token_row_count, heads_local, HEAD_SIZE), cosine, sine_table
    ).astype(jnp.bfloat16)
    key_gradient = unrotate(grad_keys_rot, cosine, sine_table).astype(jnp.bfloat16)
    joined_grad = jnp.concatenate(
        [
            grad_query.reshape(token_row_count, query_width),
            key_gradient.reshape(token_row_count, key_width),
            value_gradient.astype(jnp.bfloat16).reshape(token_row_count, key_width),
        ],
        axis=1,
    )
    normed_gradient = (
        lax.psum_scatter(
            lax.dot_general(
                w_joined, joined_grad, (((1,), (1,)), ((), ())), preferred_element_type=jnp.float32
            ).astype(jnp.bfloat16),
            "tensor",
            scatter_dimension=0,
            tiled=True,
        )
        .astype(jnp.float32)
        .T
    )
    stat = (
        lax.psum(jnp.sum(normed_gradient * gain_part[None, :] * x_float, axis=1), "tensor")
        / full_width
    )
    cubed = inverse * inverse * inverse
    grad_x = (
        grad_home.astype(jnp.float32)
        + inverse[:, None] * gain_part[None, :] * normed_gradient
        - x_float * cubed[:, None] * stat[:, None]
    )
    return (relaid, grad_x.astype(jnp.bfloat16))


def solution(mesh):
    placed = (
        P("dp", "tensor"),
        P(),
        P(None, "tensor"),
        P(None, "tensor"),
        P(None, "tensor"),
        P("tensor", None),
        P("dp", "tensor"),
        P("dp", None),
        P(),
    )
    return jax.shard_map(
        per_device,
        mesh=mesh,
        in_specs=placed,
        out_specs=(P("dp", "tensor"), P("dp", "tensor")),
        check_vma=False,
    )
```

profile of v0, /device:TPU:0, one launch (start us, length us, event | category | flops | bytes accessed | tf_op | source)
XLA Modules:
  0.0 188.4 jit_solution(454758210394766941)
XLA Ops:
  7.9 1.3 reshape.232
  11.1 1.1 reduce
  12.2 1.2 reshape.245
  13.4 7.3 %all-to-all-start.1 = ((bf16[8,2,16384]{2,1,0:T(2,128)(2,1)}), bf16[8,2,16384]{2,1,0:T(2,128)(2,1)S(1)}, u32[]{:S(2)}, u32[]{:S(2)}) async-start(bf16[8,2,16384]{2,1,0:T(2,128)(2,1)} %reshape.245), calls=%async_computation.2 | async-start | bytes 1048576 | tf_op jit(solution)/shard_map/all_to_all | solution.py:149
  21.8 7.9 %constant_dynamic-update-slice_fusion.2 = bf16[4096,1536]{1,0:T(8,128)(2,1)} fusion(bf16[4096,1024]{1,0:T(8,128)(2,1)} %param.11), kind=kLoop, calls=%fused_computation.78 | loop fusion | bytes 16777216
  29.7 1.6 constant_dynamic-update-slice_fusion.1
  32.1 1.7 constant_dynamic-update-slice_fusion
  33.8 1.4 all-to-all-done.1
  38.2 2.2 %fusion.3 = f32[256]{0:T(256)S(1)} fusion(bf16[256,4096]{1,0:T(8,128)(2,1)} %all-gather.3.cloned.1.call-done), kind=kLoop, calls=%fused_computation.11 | loop fusion | flops 3145472 | bytes 2098176 | tf_op jit(solution)/shard_map/reduce_sum | solution.py:78
  40.5 6.8 %fusion.6 = f32[256,1536]{1,0:T(8,128)S(1)} fusion(bf16[4096,1536]{1,0:T(8,128)(2,1)} %constant_dynamic-update-slice_fusion, bf16[256,4096]{1,0:T(8,128)(2,1)S(1)} %copy-done.4, f32[4096]{0:T(1024)S(1)} %copy-done.11, f32[256]{0:T(256)S(1)} %get-tuple-element.21), kind=kOutput, calls=%fused_computation.14 | convolution fusion | flops 3225419776 | bytes 16270336 | tf_op jit(solution)/shard_map/dot_general | solution.py:80
  50.1 2.1 %fusion.13 = (f32[2,4,256]{2,1,0:T(4,128)S(1)}, f32[2,256,256,4]{2,1,3,0:T(8,128)}) fusion(pred[256,256]{0,1:T(8,128)(4,1)S(1)} %fusion.34, bf16[256,2,4,64]{3,0,2,1:T(8,128)(2,1)S(1)} %bitcast.116, bf16[256,2,4,64]{3,0,2,1:T(8,128)(2,1)S(1)} %bitcast.118, bf16[256,2,64]{2,0,1:T(8,128)(2,1)S(1)} %get-tuple-element.11, ...), kind=kOutput, calls=%fused_computation.22 | convolution fusion | flops 137099264 | bytes 2826240 | tf_op jit(solution)/shard_map/qkgd,skd->kgqs/dot_general | solution.py:106
  52.2 8.0 %all-gather.5.cloned.1.call-done = bf16[256,4096]{1,0:T(8,128)(2,1)} async-done(((bf16[256,1024]{1,0:T(8,128)(2,1)}), bf16[256,4096]{1,0:T(8,128)(2,1)}) %all-gather.5.cloned.1.call-update) | async-done | bytes 2097168 | tf_op jit(solution)/shard_map/all_gather | solution.py:158
  60.2 6.4 %convolution_convert_fusion.6 = bf16[256,1024]{1,0:T(8,128)(2,1)S(1)} fusion(bf16[256,4096]{1,0:T(8,128)(2,1)} %all-gather.5.cloned.1.call-done, bf16[1024,4096]{1,0:T(8,128)(2,1)} %param.14), kind=kOutput, calls=%fused_computation.27 | convolution fusion | flops 2147745792 | bytes 11010048 | tf_op jit(solution)/shard_map/dot_general | solution.py:157
  66.8 2.4 %fusion.16 = bf16[2,128,256]{2,1,0:T(8,128)(2,1)S(1)} fusion(bf16[256,2,4,128]{0,3,2,1:T(8,128)(2,1)S(1)} %bitcast.121, f32[2,256,256,4]{2,1,3,0:T(8,128)} %get-tuple-element.23, f32[2,4,256]{2,1,0:T(4,128)S(1)} %get-tuple-element.22, pred[256,256]{0,1:T(8,128)(4,1)S(1)} %fusion.34), kind=kOutput, calls=%fused_computation.33 | convolution fusion | flops 136380416 | bytes 2826240 | tf_op jit(solution)/shard_map/kgqs,qkgd->skd/dot_general | solution.py:181
  69.3 1.6 multiply_reduce_fusion
  75.9 13.8 %convolution_convert_fusion.4 = bf16[4096,256]{0,1:T(8,128)(2,1)} fusion(bf16[4096,1536]{1,0:T(8,128)(2,1)} %constant_dynamic-update-slice_fusion, bf16[256,256]{1,0:T(8,128)(2,1)S(1)} %copy.118, bf16[256,256]{1,0:T(8,128)(2,1)S(1)} %copy-done.6, bf16[256,1024]{1,0:T(8,128)(2,1)S(1)} %bitcast.123), kind=kOutput, calls=%fused_computation.8 | convolution fusion | flops 3224633344 | bytes 15466496 | tf_op jit(solution)/shard_map/dot_general | solution.py:198
  89.8 7.1 %fusion.2 = bf16[4096,256]{0,1:T(8,128)(2,1)} fusion(bf16[256,1024]{0,1:T(8,128)(2,1)S(1)} %bitcast.120, bf16[1024,4096]{1,0:T(8,128)(2,1)} %param.14), kind=kOutput, calls=%fused_computation.10 | convolution fusion | flops 2148532224 | bytes 11010048 | tf_op jit(solution)/shard_map/dot_general | solution.py:117
  97.7 23.6 %reduce-scatter.5.cloned.1.call-done = bf16[1024,256]{0,1:T(8,128)(2,1)} async-done(((bf16[4096,256]{0,1:T(8,128)(2,1)}), bf16[1024,256]{0,1:T(8,128)(2,1)}) %reduce-scatter.5.cloned.1.call-update) | async-done | bytes 524304 | tf_op jit(solution)/shard_map/reduce_scatter | solution.py:197
  121.3 1.3 fusion.21
  122.6 5.8 %psum.7 = f32[256]{0:T(256)S(1)} all-reduce(f32[256]{0:T(256)S(1)} %fusion.21), channel_id=1, replica_groups=mesh['dp'=8,'tensor'=4] {'tensor'}, use_global_device_ids=true, to_apply=%region_11.12 | all-reduce | flops 256 | bytes 2048 | tf_op jit(solution)/shard_map/psum | solution.py:209
  128.4 26.9 %reduce-scatter.3.cloned.1.call-done = bf16[1024,256]{0,1:T(8,128)(2,1)} async-done(((bf16[4096,256]{0,1:T(8,128)(2,1)}), bf16[1024,256]{0,1:T(8,128)(2,1)}) %reduce-scatter.3.cloned.1.call-update) | async-done | bytes 524304 | tf_op jit(solution)/shard_map/reduce_scatter | solution.py:116
  155.3 2.5 %fusion.20 = (bf16[256,1024]{1,0:T(8,128)(2,1)}, bf16[256,1024]{1,0:T(8,128)(2,1)S(1)}) fusion(bf16[256,1024]{1,0:T(8,128)(2,1)S(1)} %copy-done, bf16[1024,256]{0,1:T(8,128)(2,1)} %reduce-scatter.5.cloned.1.call-done, bf16[256,1024]{1,0:T(8,128)(2,1)S(1)} %copy-done.1, f32[256]{0:T(256)S(1)} %broadcast_multiply_fusion, f32[256]{0:T(256)S(1)} %get-tuple-element.20, ...), kind=kLoop, calls=%fused_computation.37 | loop fusion | flops 3407872 | bytes 3152896 | tf_op jit(solution)/shard_map/convert_element_type | solution.py:218
  158.3 1.1 reduce.1
  159.8 19.9 %all_to_all.24 = bf16[8,2,16384]{2,1,0:T(2,128)(2,1)S(1)} all-to-all(bf16[8,2,16384]{2,1,0:T(2,128)(2,1)S(1)} %reshape.243), channel_id=1, replica_groups=mesh['dp'=8,'tensor'=4] {'dp'}, dimensions={0} | all-to-all | bytes 1048576 | tf_op jit(solution)/shard_map/all_to_all | solution.py:139
  (89 shorter events, 19.5 us)
Async XLA Ops:
  7.2 31.1 %all-gather.3.cloned.1.call-start = ((), (), s32[]{:S(2)}) async-start(), calls=%async_computation.4 | async-start | bytes 2621440 | tf_op jit(solution)/shard_map/all_gather | solution.py:76
  10.2 10.5 %copy-start.12 = (s32[1,2]{1,0:T(1,128)S(1)}, s32[1,2]{1,0:T(1,128)}, u32[]{:S(2)}) copy-start(s32[1,2]{1,0:T(1,128)} %param.16) | copy-start | bytes 28
  13.4 21.7 %all-to-all-start.1 = ((bf16[8,2,16384]{2,1,0:T(2,128)(2,1)}), bf16[8,2,16384]{2,1,0:T(2,128)(2,1)S(1)}, u32[]{:S(2)}, u32[]{:S(2)}) async-start(bf16[8,2,16384]{2,1,0:T(2,128)(2,1)} %reshape.245), calls=%async_computation.2 | async-start | bytes 1048576 | tf_op jit(solution)/shard_map/all_to_all | solution.py:149
  20.6 39.6 %all-gather.5.cloned.1.call-start = ((), (), s32[]{:S(2)}) async-start(), calls=%async_computation.6 | async-start | bytes 2621440 | tf_op jit(solution)/shard_map/all_gather | solution.py:158
  21.6 14.1 %copy-start.9 = (s32[8]{0:T(128)}, s32[8]{0:T(128)S(1)}, u32[]{:S(2)}) copy-start(s32[8]{0:T(128)S(1)} %dynamic-slice_bitcast_fusion) | copy-start | bytes 100
  21.8 45.1 %copy-start.7 = (pred[256,256]{0,1:T(8,128)(4,1)}, pred[256,256]{0,1:T(8,128)(4,1)S(1)}, u32[]{:S(2)}) copy-start(pred[256,256]{0,1:T(8,128)(4,1)S(1)} %fusion.34) | copy-start | bytes 196612
  21.8 7.9 %copy-start.2 = (bf16[4096,256]{1,0:T(8,128)(2,1)S(1)}, bf16[4096,256]{1,0:T(8,128)(2,1)}, u32[]{:S(2)}) copy-start(bf16[4096,256]{1,0:T(8,128)(2,1)} %param.12) | copy-start | bytes 6291460
  29.7 2.4 %copy-start.3 = (bf16[4096,256]{1,0:T(8,128)(2,1)S(1)}, bf16[4096,256]{1,0:T(8,128)(2,1)}, u32[]{:S(2)}) copy-start(bf16[4096,256]{1,0:T(8,128)(2,1)} %param.13) | copy-start | bytes 6291460
  36.4 4.1 %copy-start.11 = (f32[4096]{0:T(1024)S(1)}, f32[4096]{0:T(1024)}, u32[]{:S(2)}) copy-start(f32[4096]{0:T(1024)} %param.10) | copy-start | bytes 49156
  37.4 83.9 %reduce-scatter.5.cloned.1.call-start = ((), (), s32[]{:S(2)}) async-start(), calls=%async_computation.7 | async-start | bytes 2621440 | tf_op jit(solution)/shard_map/reduce_scatter | solution.py:197
  38.2 2.3 %copy-start.4 = (bf16[256,4096]{1,0:T(8,128)(2,1)S(1)}, bf16[256,4096]{1,0:T(8,128)(2,1)}, u32[]{:S(2)}) copy-start(bf16[256,4096]{1,0:T(8,128)(2,1)} %all-gather.3.cloned.1.call-done) | copy-start | bytes 6291460
  47.4 1.2 copy-start.5
  48.6 0.9 slice-start
  66.8 2.4 %copy-start.13 = (f32[2,256,256,4]{2,1,3,0:T(8,128)S(1)}, f32[2,256,256,4]{2,1,3,0:T(8,128)}, u32[]{:S(2)}) copy-start(f32[2,256,256,4]{2,1,3,0:T(8,128)} %get-tuple-element.23) | copy-start | bytes 6291460
  69.2 1.6 copy-start.8
  75.0 0.9 copy-start.6
  89.7 65.6 %reduce-scatter.3.cloned.1.call-start = ((), (), s32[]{:S(2)}) async-start(), calls=%async_computation.5 | async-start | bytes 2621440 | tf_op jit(solution)/shard_map/reduce_scatter | solution.py:116
  96.9 24.4 %copy-start = (bf16[256,1024]{1,0:T(8,128)(2,1)S(1)}, bf16[256,1024]{1,0:T(8,128)(2,1)}, u32[]{:S(2)}) copy-start(bf16[256,1024]{1,0:T(8,128)(2,1)} %param.9) | copy-start | bytes 1572868
  96.9 58.4 %copy-start.1 = (bf16[256,1024]{1,0:T(8,128)(2,1)S(1)}, bf16[256,1024]{1,0:T(8,128)(2,1)}, u32[]{:S(2)}) copy-start(bf16[256,1024]{1,0:T(8,128)(2,1)} %reshape.233) | copy-start | bytes 1572868
  155.3 2.7 %copy-start.10 = (s32[8]{0:T(128)S(1)}, s32[8]{0:T(128)}, u32[]{:S(2)}) copy-start(s32[8]{0:T(128)} %copy-done.9) | copy-start | bytes 100
Sparse Core Ops, SparseCore 0:
  9.6 25.2 all-gather.2
  37.5 22.6 all-gather.4
  89.9 31.4 reduce-scatter.4
  123.9 31.3 reduce-scatter.2
where the time goes:
time: 189 us; the launch traced here: 188 us
  waiting for transfers between devices  60.6 us (32%)
  matrix products  43.8 us (23%)
  blocking collectives  25.6 us (14%)
  local copies, waits for them, and re-layouts  25.1 us (13%)
  between operations  14.2 us (8%)
  other arithmetic  11.4 us (6%)
  starting transfers between devices  7.59 us (4%)
    reduce_scatter x1, waiting for transfers between devices, per_device(): lax.psum_scatter(lax.dot_general(w_out, attended_flat, (((0,), (1,)), (()...  26.9 us
    reduce_scatter x1, waiting for transfers between devices, per_device(): lax.psum_scatter(lax.dot_general(w_joined, joined_grad, (((1,), (1,)), ((...  23.6 us
    all_to_all x1, blocking collectives, per_device(): lax.all_to_all(outgoing, 'dp', split_axis=0, concat_axis=0, tiled=True)  19.9 us
    unnamed x39, local copies, waits for them, and re-layouts  15.5 us
    dot_general x1, matrix products, per_device(): lax.dot_general(w_joined, joined_grad, (((1,), (1,)), ((), ())), preferre...  13.8 us
    all_gather x1, waiting for transfers between devices, per_device(): lax.all_gather(grad_home, 'tensor', axis=1, tiled=True)  7.99 us
    all_to_all x1, starting transfers between devices, per_device(): lax.all_to_all(returning, 'dp', split_axis=0, concat_axis=0, tiled=True)  7.25 us
    dot_general x1, matrix products, per_device(): lax.dot_general(w_out, attended_flat, (((0,), (1,)), ((), ())), preferred...  7.11 us
  transfers between devices with their start and end apart: 5, of which 4 were waited for; matrix products, arithmetic and copies ran while one was open for 23% of the time, Pallas kernels for 0%

commit v1 on v0

--- a/solution.py
+++ b/solution.py
@@ -1,3 +1,4 @@
+import functools
 import math
 import jax
 import jax.numpy as jnp
@@ -7,6 +8,24 @@
 HEAD_SIZE = 128
 ROPE_BASE = 500000.0
 NORM_EPSILON = 1e-05
+
+
+def define_tracks(z_in, d_out):
+    a_now = lax.axis_size("tensor")
+    left_arr = lax.axis_index("tensor")
+    f_next, m_next, out_arr = (a_now, left_arr, z_in.shape[d_out])
+    even, inter = (z_in, 1)
+    while inter < f_next:
+        p_next = range(f_next)
+        piece_out = map(lambda m: (m, (m - inter) % f_next), p_next)
+        state_now = list(piece_out)
+        lower = lax.ppermute(even, "tensor", perm=state_now)
+        even = jnp.concatenate([even, lower], axis=d_out)
+        inter = 2 * inter
+    return jnp.roll(even, m_next * out_arr, axis=d_out)
+
+
+prepare_core = functools.partial(define_tracks, d_out=1)
 
 
 def doc_tables(lengths_row, token_row_count):
@@ -155,10 +174,7 @@
         .reshape(token_row_count, width_part)
     )
     attended_gradient = lax.dot_general(
-        lax.all_gather(grad_home, "tensor", axis=1, tiled=True),
-        w_out,
-        (((1,), (1,)), ((), ())),
-        preferred_element_type=jnp.float32,
+        prepare_core(grad_home), w_out, (((1,), (1,)), ((), ())), preferred_element_type=jnp.float32
     ).astype(jnp.bfloat16)
     grouped_gradient = attended_gradient.reshape(
         token_row_count, kv_local, query_group_width, HEAD_SIZE

time: 189 us -> 216 us (1.14)
  waiting for transfers between devices: 60.6 us -> 86.3 us
    ppermute x0 -> x2, waiting for transfers between devices: none -> 30.5 us  [define_tracks(): lower = lax.ppermute(even, 'tensor', perm=state_now)]
    all_gather x1 -> x0, waiting for transfers between devices: 7.99 us -> none  [per_device(): lax.all_gather(grad_home, 'tensor', axis=1, tiled=True)]
    unnamed x39 -> x42, local copies, waits for them, and re-layouts: 15.5 us -> 15.8 us
  transfers between devices with their start and end apart: 5 -> 6, of which waited for: 4 -> 5; matrix products, arithmetic and copies ran while one was open for 23% -> 15% of each run, Pallas kernels for 0% -> 0%
where the time goes in v1:
time: 216 us
  waiting for transfers between devices  86.3 us (40%)
  matrix products  42.3 us (20%)
  local copies, waits for them, and re-layouts  25.7 us (12%)
  blocking collectives  25.6 us (12%)
  between operations  14.2 us (7%)
  other arithmetic  12 us (6%)
  starting transfers between devices  9.42 us (4%)
    ppermute x2, waiting for transfers between devices, define_tracks(): lower = lax.ppermute(even, 'tensor', perm=state_now)  30.5 us
    reduce_scatter x1, waiting for transfers between devices, per_device(): lax.psum_scatter(lax.dot_general(w_out, attended_flat, (((0,), (1,)), (()...  27.1 us
    reduce_scatter x1, waiting for transfers between devices, per_device(): lax.psum_scatter(lax.dot_general(w_joined, joined_grad, (((1,), (1,)), ((...  24.7 us
    all_to_all x1, blocking collectives, per_device(): lax.all_to_all(outgoing, 'dp', split_axis=0, concat_axis=0, tiled=True)  19.9 us
    unnamed x42, local copies, waits for them, and re-layouts  15.8 us
    dot_general x1, matrix products, per_device(): lax.dot_general(w_joined, joined_grad, (((1,), (1,)), ((), ())), preferre...  13.8 us
    all_to_all x1, starting transfers between devices, per_device(): lax.all_to_all(returning, 'dp', split_axis=0, concat_axis=0, tiled=True)  7.25 us
    dot_general x1, matrix products, per_device(): lax.dot_general(w_out, attended_flat, (((0,), (1,)), ((), ())), preferred...  7.11 us
  transfers between devices with their start and end apart: 6, of which 5 were waited for; matrix products, arithmetic and copies ran while one was open for 15% of the time, Pallas kernels for 0%

profile of v1, /device:TPU:0, one launch (start us, length us, event | category | flops | bytes accessed | tf_op | source)
XLA Modules:
  0.0 215.6 jit_solution(16107321229920165121)
XLA Ops:
  12.6 7.3 %all-to-all-start.1 = ((bf16[8,2,16384]{2,1,0:T(2,128)(2,1)}), bf16[8,2,16384]{2,1,0:T(2,128)(2,1)S(1)}, u32[]{:S(2)}, u32[]{:S(2)}) async-start(bf16[8,2,16384]{2,1,0:T(2,128)(2,1)} %reshape.245), calls=%async_computation.2 | async-start | bytes 1048576 | tf_op jit(solution)/shard_map/all_to_all | solution.py:168
  21.5 7.9 %constant_dynamic-update-slice_fusion.2 = bf16[4096,1536]{1,0:T(8,128)(2,1)} fusion(bf16[4096,1024]{1,0:T(8,128)(2,1)} %param.11), kind=kLoop, calls=%fused_computation.81 | loop fusion | bytes 16777216
  29.4 1.7 constant_dynamic-update-slice_fusion.1
  31.1 3.2 %all-to-all-done.1 = bf16[8,2,16384]{2,1,0:T(2,128)(2,1)S(1)} async-done(((bf16[8,2,16384]{2,1,0:T(2,128)(2,1)}), bf16[8,2,16384]{2,1,0:T(2,128)(2,1)S(1)}, u32[]{:S(2)}, u32[]{:S(2)}) %all-to-all-start.1) | async-done | bytes 524320 | tf_op jit(solution)/shard_map/all_to_all | solution.py:168
  34.9 1.5 convolution_convert_fusion
  36.4 1.4 reshape.233
  38.7 9.5 %collective-permute-done = bf16[256,1024]{1,0:T(8,128)(2,1)S(1)} collective-permute-done((bf16[256,1024]{1,0:T(8,128)(2,1)S(1)}, bf16[256,1024]{1,0:T(8,128)(2,1)S(1)}, u32[]{:S(2)}, u32[]{:S(2)}) %collective-permute-start) | collective-permute-done | bytes 524320 | tf_op jit(solution)/shard_map/ppermute | solution.py:22
  48.3 1.8 collective-permute-start.1
  50.6 1.6 constant_dynamic-update-slice_fusion
  52.4 21.0 %collective-permute-done.1 = bf16[256,2048]{1,0:T(8,128)(2,1)S(1)} collective-permute-done((bf16[256,2048]{1,0:T(8,128)(2,1)S(1)}, bf16[256,2048]{1,0:T(8,128)(2,1)S(1)}, u32[]{:S(2)}, u32[]{:S(2)}) %collective-permute-start.1) | collective-permute-done | bytes 1048608 | tf_op jit(solution)/shard_map/ppermute | solution.py:22
  73.6 5.7 %fusion.16 = bf16[256,1024]{1,0:T(8,128)(2,1)S(1)} fusion(bf16[1024,4096]{1,0:T(8,128)(2,1)} %param.14, bf16[256,8192]{1,0:T(8,128)(2,1)S(1)} %constant_dynamic-update-slice_fusion.3, s32[]{:T(128)S(6)} %select_n.32), kind=kOutput, calls=%fused_computation.29 | convolution fusion | flops 2147745792 | bytes 11010052 | tf_op jit(solution)/shard_map/dot_general | solution.py:176
  79.6 2.2 %fusion.3 = f32[256]{0:T(256)S(1)} fusion(bf16[256,4096]{1,0:T(8,128)(2,1)} %all-gather.2.cloned.1.call-done), kind=kLoop, calls=%fused_computation.11 | loop fusion | flops 3145472 | bytes 2098176 | tf_op jit(solution)/shard_map/reduce_sum | solution.py:97
  81.9 6.7 %fusion.6 = f32[256,1536]{1,0:T(8,128)S(1)} fusion(bf16[4096,1536]{1,0:T(8,128)(2,1)} %constant_dynamic-update-slice_fusion, bf16[256,4096]{1,0:T(8,128)(2,1)S(1)} %copy-done.3, f32[4096]{0:T(1024)S(1)} %copy-done.11, f32[256]{0:T(256)S(1)} %get-tuple-element.21), kind=kOutput, calls=%fused_computation.14 | convolution fusion | flops 3225419776 | bytes 16270336 | tf_op jit(solution)/shard_map/dot_general | solution.py:99
  91.4 1.7 fusion.15
  93.1 1.3 fusion.21
  94.4 1.5 multiply_reduce_fusion
  101.0 13.8 %convolution_convert_fusion.4 = bf16[4096,256]{0,1:T(8,128)(2,1)} fusion(bf16[4096,1536]{1,0:T(8,128)(2,1)} %constant_dynamic-update-slice_fusion, bf16[256,256]{1,0:T(8,128)(2,1)S(1)} %copy.118, bf16[256,256]{1,0:T(8,128)(2,1)S(1)} %copy-done.6, bf16[256,1024]{1,0:T(8,128)(2,1)S(1)} %bitcast.122), kind=kOutput, calls=%fused_computation.8 | convolution fusion | flops 3224633344 | bytes 15466496 | tf_op jit(solution)/shard_map/dot_general | solution.py:214
  115.8 7.1 %fusion.2 = bf16[4096,256]{0,1:T(8,128)(2,1)} fusion(bf16[256,1024]{0,1:T(8,128)(2,1)S(1)} %bitcast.119, bf16[1024,4096]{1,0:T(8,128)(2,1)} %param.14), kind=kOutput, calls=%fused_computation.10 | convolution fusion | flops 2148532224 | bytes 11010048 | tf_op jit(solution)/shard_map/dot_general | solution.py:136
  123.7 24.7 %reduce-scatter.5.cloned.1.call-done = bf16[1024,256]{0,1:T(8,128)(2,1)} async-done(((bf16[4096,256]{0,1:T(8,128)(2,1)}), bf16[1024,256]{0,1:T(8,128)(2,1)}) %reduce-scatter.5.cloned.1.call-update) | async-done | bytes 524304 | tf_op jit(solution)/shard_map/reduce_scatter | solution.py:213
  148.5 1.3 fusion.26
  149.7 5.8 %psum.7 = f32[256]{0:T(256)S(1)} all-reduce(f32[256]{0:T(256)S(1)} %fusion.26), channel_id=1, replica_groups=mesh['dp'=8,'tensor'=4] {'tensor'}, use_global_device_ids=true, to_apply=%region_11.12 | all-reduce | flops 256 | bytes 2048 | tf_op jit(solution)/shard_map/psum | solution.py:225
  155.5 27.1 %reduce-scatter.3.cloned.1.call-done = bf16[1024,256]{0,1:T(8,128)(2,1)} async-done(((bf16[4096,256]{0,1:T(8,128)(2,1)}), bf16[1024,256]{0,1:T(8,128)(2,1)}) %reduce-scatter.3.cloned.1.call-update) | async-done | bytes 524304 | tf_op jit(solution)/shard_map/reduce_scatter | solution.py:135
  182.6 2.5 %fusion.25 = (bf16[256,1024]{1,0:T(8,128)(2,1)}, bf16[256,1024]{1,0:T(8,128)(2,1)S(1)}) fusion(bf16[256,1024]{1,0:T(8,128)(2,1)S(1)} %copy-done, bf16[1024,256]{0,1:T(8,128)(2,1)} %reduce-scatter.5.cloned.1.call-done, bf16[256,1024]{1,0:T(8,128)(2,1)S(1)} %reshape.233, f32[256]{0:T(256)S(1)} %broadcast_multiply_fusion, f32[256]{0:T(256)S(1)} %get-tuple-element.20, ...), kind=kLoop, calls=%fused_computation.39 | loop fusion | flops 3407872 | bytes 3152896 | tf_op jit(solution)/shard_map/convert_element_type | solution.py:234
  187.0 19.9 %all_to_all.24 = bf16[8,2,16384]{2,1,0:T(2,128)(2,1)S(1)} all-to-all(bf16[8,2,16384]{2,1,0:T(2,128)(2,1)S(1)} %reshape.243), channel_id=1, replica_groups=mesh['dp'=8,'tensor'=4] {'dp'}, dimensions={0} | all-to-all | bytes 1048576 | tf_op jit(solution)/shard_map/all_to_all | solution.py:158
  (95 shorter events, 23.2 us)
Async XLA Ops:
  9.8 11.5 %copy-start.12 = (s32[1,2]{1,0:T(1,128)S(1)}, s32[1,2]{1,0:T(1,128)}, u32[]{:S(2)}) copy-start(s32[1,2]{1,0:T(1,128)} %param.16) | copy-start | bytes 28
  12.6 21.7 %all-to-all-start.1 = ((bf16[8,2,16384]{2,1,0:T(2,128)(2,1)}), bf16[8,2,16384]{2,1,0:T(2,128)(2,1)S(1)}, u32[]{:S(2)}, u32[]{:S(2)}) async-start(bf16[8,2,16384]{2,1,0:T(2,128)(2,1)} %reshape.245), calls=%async_computation.2 | async-start | bytes 1048576 | tf_op jit(solution)/shard_map/all_to_all | solution.py:168
  19.9 59.8 %all-gather.2.cloned.1.call-start = ((), (), s32[]{:S(2)}) async-start(), calls=%async_computation.4 | async-start | bytes 2621440 | tf_op jit(solution)/shard_map/all_gather | solution.py:95
  20.6 127.9 %reduce-scatter.5.cloned.1.call-start = ((), (), s32[]{:S(2)}) async-start(), calls=%async_computation.6 | async-start | bytes 2621440 | tf_op jit(solution)/shard_map/reduce_scatter | solution.py:213
  21.3 13.5 %copy-start.9 = (s32[8]{0:T(128)}, s32[8]{0:T(128)S(1)}, u32[]{:S(2)}) copy-start(s32[8]{0:T(128)S(1)} %dynamic-slice_bitcast_fusion) | copy-start | bytes 100
  21.5 7.9 %copy-start.1 = (bf16[4096,256]{1,0:T(8,128)(2,1)S(1)}, bf16[4096,256]{1,0:T(8,128)(2,1)}, u32[]{:S(2)}) copy-start(bf16[4096,256]{1,0:T(8,128)(2,1)} %param.12) | copy-start | bytes 6291460
  36.4 14.3 %copy-start.2 = (bf16[4096,256]{1,0:T(8,128)(2,1)S(1)}, bf16[4096,256]{1,0:T(8,128)(2,1)}, u32[]{:S(2)}) copy-start(bf16[4096,256]{1,0:T(8,128)(2,1)} %param.13) | copy-start | bytes 6291460
  37.8 10.4 %collective-permute-start = (bf16[256,1024]{1,0:T(8,128)(2,1)S(1)}, bf16[256,1024]{1,0:T(8,128)(2,1)S(1)}, u32[]{:S(2)}, u32[]{:S(2)}) collective-permute-start(bf16[256,1024]{1,0:T(8,128)(2,1)S(1)} %reshape.233), channel_id=1, source_target_pairs={{0,3},{1,0},{2,1},{3,2},{4,7},{5,4},{6,5},{7,6},{8,11},{9,8},{10,9... | collective-permute-start | bytes 1572872 | tf_op jit(solution)/shard_map/ppermute | solution.py:22
  48.3 25.1 %collective-permute-start.1 = (bf16[256,2048]{1,0:T(8,128)(2,1)S(1)}, bf16[256,2048]{1,0:T(8,128)(2,1)S(1)}, u32[]{:S(2)}, u32[]{:S(2)}) collective-permute-start(bf16[256,2048]{1,0:T(8,128)(2,1)S(1)} %pad_maximum_fusion), channel_id=1, source_target_pairs={{0,2},{1,3},{2,0},{3,1},{4,6},{5,7},{6,4},{7,5},{8,10},{9,11},{10,... | collective-permute-start | bytes 3145736 | tf_op jit(solution)/shard_map/ppermute | solution.py:22
  79.4 2.5 %copy-start.11 = (f32[4096]{0:T(1024)S(1)}, f32[4096]{0:T(1024)}, u32[]{:S(2)}) copy-start(f32[4096]{0:T(1024)} %param.10) | copy-start | bytes 49156
  79.6 2.3 %copy-start.3 = (bf16[256,4096]{1,0:T(8,128)(2,1)S(1)}, bf16[256,4096]{1,0:T(8,128)(2,1)}, u32[]{:S(2)}) copy-start(bf16[256,4096]{1,0:T(8,128)(2,1)} %all-gather.2.cloned.1.call-done) | copy-start | bytes 6291460
  88.6 1.2 copy-start.4
  89.8 0.9 slice-start
  91.3 1.8 copy-start.8
  96.6 1.0 copy-start.7
  100.1 0.9 copy-start.6
  114.8 1.0 copy-start.5
  114.8 67.8 %reduce-scatter.3.cloned.1.call-start = ((), (), s32[]{:S(2)}) async-start(), calls=%async_computation.5 | async-start | bytes 2621440 | tf_op jit(solution)/shard_map/reduce_scatter | solution.py:135
  123.0 25.5 %copy-start = (bf16[256,1024]{1,0:T(8,128)(2,1)S(1)}, bf16[256,1024]{1,0:T(8,128)(2,1)}, u32[]{:S(2)}) copy-start(bf16[256,1024]{1,0:T(8,128)(2,1)} %param.9) | copy-start | bytes 1572868
  182.6 2.7 %copy-start.10 = (s32[8]{0:T(128)S(1)}, s32[8]{0:T(128)}, u32[]{:S(2)}) copy-start(s32[8]{0:T(128)} %copy-done.9) | copy-start | bytes 100
Sparse Core Ops, SparseCore 0:
  22.2 26.0 all-gather.1
  115.0 33.4 reduce-scatter.4
  151.1 31.4 reduce-scatter.2
